TPU v7x, 512 devices: a whole 4x4x16 slice. The times are simulated.
512 devices in a mesh: front: 4 (over y), row: 4 (over x), col: 32 (over z, core).
Axes of the slice: x: 4, y: 4, z: 16, core: 2. Of those that a mesh axis runs over, the one named last changes fastest.
Arguments:
- inverse_factor: bfloat16 [4, 1024, 1024], P('front', ('row', 'col')), as said below
- panel: bfloat16 [4, 8192, 1024], P('front', 'row', 'col'), may hold values from -1.1953125 to 1.1953125
- trailing: float32 [4, 8192, 8192], P('front', 'row', 'col'), may hold values from -6 to 6
- extend_map: int32 [4, 512], P('front'), may hold values from 0 to 511, as said below
Outputs:
- parent_update: float32 [4, 4096, 8192], P('front', 'row', 'col')
Inputs may be any that keep to these rules, and one draw needn't show every extreme that they name: Each inverse_factor[f] is upper triangular with positive diagonal. Each row of extend_map is a permutation of 0 to 511, and extend_map[f, q] % (128) == q % 128.
All inputs are finite; a program needn't handle non-finite values.
Results may differ from a plain program's by a relative error of at most 0.0034.
Values may be sent and summed in bfloat16 or wider, within the bound.
No kernel may reach another device: no remote copies, remote signals or barrier semaphores. Data moves between devices by JAX's collectives and lax.ppermute only.
A program may use at most 64 MiB of HBM per device.

v0:
```python
import jax
import jax.numpy as jnp
from jax import lax
from jax.sharding import Mesh
from jax.sharding import PartitionSpec as P


def from_partner(value, axis, distance):
    mask = 2**distance
    pairs = [(source, source ^ mask) for source in range(lax.axis_size(axis))]
    return lax.ppermute(value, axis, pairs)


def outer_rows(left, right):
    return lax.dot_general(
        left, right, (((1,), (1,)), ((), ())), preferred_element_type=jnp.float32
    )


def local(inverse_factor, panel, trailing, extend_map):
    nrow = lax.axis_size("row")
    nz = lax.axis_size("z")
    ncore = lax.axis_size("core")
    ncol = nz * ncore
    group = nrow * ncol
    row_index = lax.axis_index("row")
    col_index = lax.axis_index("z") * ncore + lax.axis_index("core")
    inverse = lax.all_gather(inverse_factor[0], "core", axis=0, tiled=True)
    inverse = lax.all_gather(inverse, "z", axis=0, tiled=True)
    inverse = lax.all_gather(inverse, "row", axis=0, tiled=True)
    order = inverse.shape[0]
    chunk = order // ncol
    inverse = inverse.reshape(nz, ncore, chunk, order).transpose(1, 0, 2, 3).reshape(order, order)
    columns = lax.all_gather(panel[0], "z", axis=1, tiled=True)
    columns = lax.all_gather(columns, "core", axis=1, tiled=True)
    solved = jnp.dot(columns, inverse, preferred_element_type=jnp.float32).astype(jnp.bfloat16)
    local_trailing = trailing[0]
    rows_here = local_trailing.shape[0]
    cols_here = local_trailing.shape[1]
    share = rows_here // ncol
    piece = lax.dynamic_slice_in_dim(solved, col_index * share, share, 0)
    col_side = lax.all_gather(piece, "row", axis=0, tiled=True)
    block_map = extend_map[0]
    nblocks = block_map.shape[0]
    per_class = nblocks // group
    width = rows_here // (ncol * per_class)
    slots_row = jnp.arange(ncol * per_class, dtype=jnp.int32)
    class_row = slots_row // per_class
    depth_row = slots_row % per_class
    source_row = (depth_row * ncol + class_row) * nrow + row_index
    target_row = class_row * per_class + block_map[source_row] // group
    gather_row = jnp.argsort(target_row)
    slots_col = jnp.arange(nrow * per_class, dtype=jnp.int32)
    class_col = slots_col // per_class
    depth_col = slots_col % per_class
    source_col = (depth_col * ncol + col_index) * nrow + class_col
    target_col = class_col * per_class + block_map[source_col] // group
    gather_col = jnp.argsort(target_col)
    col_side = col_side.reshape(nrow * per_class, width, order)[gather_col].reshape(
        cols_here, order
    )
    lane = jnp.arange(cols_here, dtype=jnp.int32)
    picked = gather_col[lane // width] * width + lane % width
    select_cols = (lane[:, None] == picked[None, :]).astype(jnp.float32)
    member = lax.axis_index("front") % 2
    half = rows_here // 2
    half_blocks = half // width

    def half_update(which):
        rows = lax.dynamic_slice_in_dim(local_trailing, which * half, half, 0)
        low = lax.dynamic_slice_in_dim(solved, which * half, half, 0)
        moved_cols = jnp.dot(
            rows, select_cols, precision=lax.Precision.HIGHEST, preferred_element_type=jnp.float32
        )
        schur = moved_cols - outer_rows(low, col_side)
        blocks = (
            lax.dynamic_slice_in_dim(gather_row, which * half_blocks, half_blocks, 0)
            - which * half_blocks
        )
        return schur.reshape(half_blocks, width, cols_here)[blocks].reshape(half, cols_here)

    outgoing = half_update(1 - member)
    incoming = from_partner(outgoing, "front", 0)
    keep = half_update(member)
    return (keep + incoming)[None]


def solution(mesh):
    devices = mesh.devices
    shape = devices.shape
    fine = Mesh(
        devices.reshape(shape[0], shape[1], shape[2] // 2, 2), ("front", "row", "z", "core")
    )
    cols = ("z", "core")
    return jax.shard_map(
        local,
        mesh=fine,
        in_specs=(
            P("front", ("row",) + cols, None),
            P("front", "row", cols),
            P("front", "row", cols),
            P("front", None),
        ),
        out_specs=P("front", "row", cols),
        check_vma=False,
    )
```

profile of v0, /device:TPU:8, one launch (start us, length us, event | category | flops | bytes accessed | tf_op | source)
XLA Modules:
  0.0 213.7 jit_solution(8595470988300910653)
XLA Ops:
  6.5 0.7 all-gather.9.cloned.1.call-update
  7.3 2.0 all-gather.2
  9.3 42.3 %all-gather.3 = bf16[1,256,1024]{2,1,0:T(8,128)(2,1)} all-gather(bf16[1,16,1024]{2,1,0:T(8,128)(2,1)S(1)} %all-gather.2), channel_id=5, replica_groups=mesh['front'=4,'row'=4,'z'=16,'core'=2] {'z'}, dimensions={1}, use_global_device_ids=true | all-gather | bytes 557056 | tf_op jit(solution)/shard_map/all_gather | solution.py:29
  51.7 35.8 %all-gather.9.cloned.1.call-done = bf16[1,2048,512]{1,2,0:T(8,128)(2,1)} async-done(((bf16[1,2048,32]{1,2,0:T(8,128)(2,1)}), bf16[1,2048,512]{1,2,0:T(8,128)(2,1)}) %all-gather.9.cloned.1.call-update) | async-done | bytes 2097168 | tf_op jit(solution)/shard_map/all_gather | solution.py:34
  88.2 1.3 gather_fusion.2
  89.6 1.2 sort.34
  90.8 2.5 %sort.35 = (s32[128]{0:T(128)}, s32[128]{0:T(128)S(1)}) sort(s32[128]{0:T(128)S(1)} %fusion.28, s32[128]{0:T(128)S(1)} %iota.41), dimensions={0}, to_apply=%region_1.2 | sort | flops 896 | bytes 2048 | tf_op jit(solution)/shard_map/jit(argsort)/sort | solution.py:52
  93.6 0.7 fusion.34
  94.3 4.2 %compare_select_fusion.1 = s32[256,1]{0,1:T(1,128)S(1)} fusion(s32[]{:T(128)} %bitcast.12, s32[]{:T(128)} %bitcast.13, s32[]{:T(128)} %bitcast.14, s32[]{:T(128)} %bitcast.15, s32[]{:T(128)} %bitcast.16, s32[]{:T(128)} %bitcast.18, s32[]{:T(128)} %bitcast.17), kind=kLoop, calls=%fused_computation.37 | loop fusion | flops 5888 | bytes 1052 | tf_op jit(solution)/shard_map/gather | solution.py:63
  98.5 5.6 %fusion.19 = s32[256]{0:T(256)S(1)} fusion(pred[256]{0:T(512)(128)(4,1)S(1)} %get-tuple-element.27, pred[256]{0:T(512)(128)(4,1)S(1)} %get-tuple-element.28, pred[256]{0:T(512)(128)(4,1)S(1)} %get-tuple-element.29, pred[256]{0:T(512)(128)(4,1)S(1)} %get-tuple-element.30, pred[256]{0:T(512)(128)(4,1)S(1)} %get-tuple-element.31, ...), kind=kLoop, calls=%fused_computation.72 | loop fusion | flops 4352 | bytes 4388 | tf_op jit(solution)/shard_map/add | solution.py:63
  104.1 21.1 %all-gather.13.cloned.1.call-done = bf16[1,1024,1024]{2,1,0:T(8,128)(2,1)} async-done(((bf16[1,256,1024]{2,1,0:T(8,128)(2,1)}), bf16[1,1024,1024]{2,1,0:T(8,128)(2,1)}) %all-gather.13.cloned.1.call-update) | async-done | bytes 2097168 | tf_op jit(solution)/shard_map/all_gather | solution.py:30
  125.2 3.3 %copy.5 = bf16[2,16,32,1024]{3,2,1,0:T(8,128)(2,1)} copy(bf16[2,16,32,1024]{3,2,0,1:T(8,128)(2,1)} %bitcast.54) | data formatting | bytes 4194304 | tf_op jit(solution)/shard_map/transpose | solution.py:33
  128.4 23.1 %all-gather.11.cloned.1.call-done = bf16[1,2048,1024]{1,2,0:T(8,128)(2,1)} async-done(((bf16[1,2048,512]{1,2,0:T(8,128)(2,1)}), bf16[1,2048,1024]{1,2,0:T(8,128)(2,1)}) %all-gather.11.cloned.1.call-update) | async-done | bytes 4194320 | tf_op jit(solution)/shard_map/all_gather | solution.py:35
  151.5 7.4 %fusion.2 = bf16[2048,1024]{1,0:T(8,128)(2,1)S(1)} fusion(bf16[1024,1024]{1,0:T(8,128)(2,1)} %bitcast.55, bf16[1,2048,1024]{1,2,0:T(8,128)(2,1)} %all-gather.11.cloned.1.call-done), kind=kOutput, calls=%fused_computation.7 | convolution fusion | flops 4297064448 | bytes 10485760 | tf_op jit(solution)/shard_map/dot_general | solution.py:36
  159.0 13.1 %all_gather.23 = bf16[256,1024]{1,0:T(8,128)(2,1)S(1)} all-gather(bf16[64,1024]{1,0:T(8,128)(2,1)S(1)} %constant_dynamic-slice_fusion), channel_id=1, replica_groups=mesh['front'=4,'row'=4,'z'=16,'core'=2] {'row'}, dimensions={0}, use_global_device_ids=true | all-gather | bytes 655360 | tf_op jit(solution)/shard_map/all_gather | solution.py:42
  172.7 2.3 %fusion.5 = f32[1024,256]{1,0:T(8,128)S(1)} fusion(bf16[256,1024]{1,0:T(8,128)(2,1)S(1)} %bitcast.50, bf16[2048,1024]{1,0:T(8,128)(2,1)} %copy-done.2, s32[]{:T(128)S(6)} %select_n.164), kind=kOutput, calls=%fused_computation.8 | convolution fusion | flops 536870912 | bytes 3670020 | tf_op jit(solution)/shard_map/dot_general | solution.py:15
  175.1 1.6 convolution_subtract_fusion
  176.7 2.8 %gather_fusion.4 = f32[64,16,256]{2,1,0:T(8,128)} fusion(f32[64,16,256]{2,1,0:T(8,128)} %bitcast.53, s32[1024]{0:T(1024)S(1)} %pad_clamp_fusion), kind=kCustom, calls=%fused_computation.4 | custom fusion | bytes 2097408 | tf_op jit(solution)/shard_map/gather | solution.py:80
  179.5 3.1 %collective-permute-start = (f32[1024,256]{1,0:T(8,128)}, f32[1024,256]{1,0:T(8,128)}, u32[]{:S(2)}, u32[]{:S(2)}) collective-permute-start(f32[1024,256]{1,0:T(8,128)} %bitcast.57), channel_id=1, source_target_pairs={{0,128},{128,0},{256,384},{384,256},{1,129},{129,1},{257,385},{385... | collective-permute-start | bytes 3145736 | tf_op jit(solution)/shard_map/ppermute | solution.py:11
  182.7 2.3 %fusion.7 = f32[1024,256]{1,0:T(8,128)S(1)} fusion(bf16[256,1024]{1,0:T(8,128)(2,1)S(1)} %bitcast.51, bf16[2048,1024]{1,0:T(8,128)(2,1)} %copy-done.2, s32[]{:T(128)S(6)} %select_n.146), kind=kOutput, calls=%fused_computation.10 | convolution fusion | flops 536870912 | bytes 3670020 | tf_op jit(solution)/shard_map/dot_general | solution.py:15
  185.0 1.6 convolution_subtract_fusion.1
  186.6 1.8 gather_fusion.3
  188.5 16.4 %collective-permute-done = f32[1024,256]{1,0:T(8,128)} collective-permute-done((f32[1024,256]{1,0:T(8,128)}, f32[1024,256]{1,0:T(8,128)}, u32[]{:S(2)}, u32[]{:S(2)}) %collective-permute-start) | collective-permute-done | bytes 1048608 | tf_op jit(solution)/shard_map/ppermute | solution.py:11
  204.9 2.3 %bitcast_add_fusion = f32[1024,256]{1,0:T(8,128)} fusion(f32[1024,256]{1,0:T(8,128)} %collective-permute-done, f32[64,16,256]{2,1,0:T(8,128)S(1)} %gather_fusion.3), kind=kLoop, calls=%fused_computation.15 | loop fusion | flops 262144 | bytes 3145728 | tf_op jit(solution)/shard_map/add | solution.py:85
  (32 shorter events, 1.7 us)
Async XLA Ops:
  6.5 168.5 %copy-start = (f32[1,2048,256]{2,1,0:T(8,128)S(1)}, f32[1,2048,256]{2,1,0:T(8,128)}, u32[]{:S(2)}) copy-start(f32[1,2048,256]{2,1,0:T(8,128)} %param.6) | copy-start | bytes 6291460
  6.5 81.0 %copy-start.1 = (s32[1,512]{1,0:T(1,128)S(1)}, s32[1,512]{1,0:T(1,128)}, u32[]{:S(2)}) copy-start(s32[1,512]{1,0:T(1,128)} %param.7) | copy-start | bytes 6148
  6.5 80.9 %all-gather.9.cloned.1.call-start = ((), (), s32[]{:S(2)}) async-start(), calls=%async_computation | async-start | bytes 2228224 | tf_op jit(solution)/shard_map/all_gather | solution.py:34
  7.3 117.9 %all-gather.13.cloned.1.call-start = ((), (), s32[]{:S(2)}) async-start(), calls=%async_computation.2 | async-start | bytes 2621440 | tf_op jit(solution)/shard_map/all_gather | solution.py:30
  51.7 99.9 %all-gather.11.cloned.1.call-start = ((), (), s32[]{:S(2)}) async-start(), calls=%async_computation.1 | async-start | bytes 6291456 | tf_op jit(solution)/shard_map/all_gather | solution.py:35
  159.0 13.2 %copy-start.2 = (bf16[2048,1024]{1,0:T(8,128)(2,1)}, bf16[2048,1024]{1,0:T(8,128)(2,1)S(1)}, u32[]{:S(2)}) copy-start(bf16[2048,1024]{1,0:T(8,128)(2,1)S(1)} %fusion.2) | copy-start | bytes 12582916
  179.5 25.4 %collective-permute-start = (f32[1024,256]{1,0:T(8,128)}, f32[1024,256]{1,0:T(8,128)}, u32[]{:S(2)}, u32[]{:S(2)}) collective-permute-start(f32[1024,256]{1,0:T(8,128)} %bitcast.57), channel_id=1, source_target_pairs={{0,128},{128,0},{256,384},{384,256},{1,129},{129,1},{257,385},{385... | collective-permute-start | bytes 3145736 | tf_op jit(solution)/shard_map/ppermute | solution.py:11
Sparse Core Ops, SparseCore 0:
  9.4 77.9 all-gather.8
  89.6 35.5 all-gather.12
  127.2 24.2 all-gather.10
where the time goes:
time: 214 us
  waiting for transfers between devices  97.1 us (45%)
  blocking collectives  57.4 us (27%)
  other arithmetic  16.1 us (8%)
  matrix products  15.4 us (7%)
  between operations  13.3 us (6%)
  local copies, waits for them, and re-layouts  11.2 us (5%)
  starting transfers between devices  3.22 us (2%)
    all_gather x1, blocking collectives, local(): inverse = lax.all_gather(inverse, 'z', axis=0, tiled=True)  42.3 us
    all_gather x1, waiting for transfers between devices, local(): columns = lax.all_gather(panel[0], 'z', axis=1, tiled=True)  35.8 us
    all_gather x1, waiting for transfers between devices, local(): columns = lax.all_gather(columns, 'core', axis=1, tiled=True)  23.1 us
    all_gather x1, waiting for transfers between devices, local(): inverse = lax.all_gather(inverse, 'row', axis=0, tiled=True)  21.1 us
    ppermute x1, waiting for transfers between devices, from_partner(): return lax.ppermute(value, axis, pairs)  16.4 us
    all_gather x1, blocking collectives, local(): col_side = lax.all_gather(piece, 'row', axis=0, tiled=True)  13.1 us
    dot_general x1, matrix products, local(): jnp.dot(columns, inverse, preferred_element_type=jnp.float32)  7.43 us
    add x1, other arithmetic, local(): picked = gather_col[lane // width] * width + lane % width  5.58 us
  transfers between devices with their start and end apart: 4, of which 4 were waited for; matrix products, arithmetic and copies ran while one was open for 12% of the time, Pallas kernels for 0%

commit v1 on v0

--- a/solution.py
+++ b/solution.py
@@ -31,7 +31,10 @@
     order = inverse.shape[0]
     chunk = order // ncol
     inverse = inverse.reshape(nz, ncore, chunk, order).transpose(1, 0, 2, 3).reshape(order, order)
-    columns = lax.all_gather(panel[0], "z", axis=1, tiled=True)
+    mat = panel[0]
+    top = jnp.stack(jax.lax.psum(1, axis_name="z") * [mat], axis=0)
+    a_next = jax.lax.all_to_all(top, axis_name="z", split_axis=0, concat_axis=0)
+    columns = jnp.concatenate(a_next, 1)
     columns = lax.all_gather(columns, "core", axis=1, tiled=True)
     solved = jnp.dot(columns, inverse, preferred_element_type=jnp.float32).astype(jnp.bfloat16)
     local_trailing = trailing[0]

time: 214 us -> 273 us (1.28)
  blocking collectives: 57.4 us -> 135 us
  waiting for transfers between devices: 97.1 us -> 60.3 us
  starting transfers between devices: 3.22 us -> 18.6 us
    all_gather x1, blocking collectives: 42.3 us -> 120 us  [local(): inverse = lax.all_gather(inverse, 'z', axis=0, tiled=True)]
    all_gather x1 -> x0, waiting for transfers between devices: 35.8 us -> none  [local(): columns = lax.all_gather(panel[0], 'z', axis=1, tiled=True)]
    all_to_all x0 -> x1, starting transfers between devices: none -> 15.4 us  [local(): a_next = jax.lax.all_to_all(top, axis_name='z', split_axis=0, concat_axis=0)]
  transfers between devices with their start and end apart: 4 -> 4, of which waited for: 4 -> 3; matrix products, arithmetic and copies ran while one was open for 12% -> 9% of each run, Pallas kernels for 0% -> 0%
where the time goes in v1:
time: 273 us
  blocking collectives  135 us (49%)
  waiting for transfers between devices  60.3 us (22%)
  starting transfers between devices  18.6 us (7%)
  other arithmetic  16.1 us (6%)
  matrix products  15.4 us (6%)
  local copies, waits for them, and re-layouts  13.8 us (5%)
  between operations  13.7 us (5%)
    all_gather x1, blocking collectives, local(): inverse = lax.all_gather(inverse, 'z', axis=0, tiled=True)  120 us
    all_gather x1, waiting for transfers between devices, local(): columns = lax.all_gather(columns, 'core', axis=1, tiled=True)  23.1 us
    all_gather x1, waiting for transfers between devices, local(): inverse = lax.all_gather(inverse, 'row', axis=0, tiled=True)  20.1 us
    ppermute x1, waiting for transfers between devices, from_partner(): return lax.ppermute(value, axis, pairs)  16.4 us
    all_to_all x1, starting transfers between devices, local(): a_next = jax.lax.all_to_all(top, axis_name='z', split_axis=0, concat_axis=0)  15.4 us
    all_gather x1, blocking collectives, local(): col_side = lax.all_gather(piece, 'row', axis=0, tiled=True)  13.1 us
    dot_general x1, matrix products, local(): jnp.dot(columns, inverse, preferred_element_type=jnp.float32)  7.43 us
    add x1, other arithmetic, local(): picked = gather_col[lane // width] * width + lane % width  5.58 us
  transfers between devices with their start and end apart: 4, of which 3 were waited for; matrix products, arithmetic and copies ran while one was open for 9% of the time, Pallas kernels for 0%

profile of v1, /device:TPU:8, one launch (start us, length us, event | category | flops | bytes accessed | tf_op | source)
XLA Modules:
  0.0 272.7 jit_solution(5347156305078598061)
XLA Ops:
  6.5 2.7 stack.3
  9.2 15.4 %all-to-all-start = ((bf16[16,2048,32]{1,2,0:T(8,128)(2,1)}), bf16[16,2048,32]{1,2,0:T(8,128)(2,1)}, u32[]{:S(2)}, u32[]{:S(2)}) async-start(bf16[16,2048,32]{1,2,0:T(8,128)(2,1)} %stack.3), calls=%async_computation | async-start | bytes 4194304 | tf_op jit(solution)/shard_map/all_to_all | solution.py:36
  24.7 1.8 all-gather
  26.5 119.8 %all-gather.1 = bf16[1,256,1024]{2,1,0:T(8,128)(2,1)} all-gather(bf16[1,16,1024]{2,1,0:T(8,128)(2,1)S(1)} %all-gather), channel_id=3, replica_groups=mesh['front'=4,'row'=4,'z'=16,'core'=2] {'z'}, dimensions={1}, use_global_device_ids=true | all-gather | bytes 557056 | tf_op jit(solution)/shard_map/all_gather | solution.py:29
  147.9 1.3 gather_fusion.2
  149.2 1.2 sort.34
  150.4 2.5 sort.35
  153.2 0.7 fusion.29
  153.9 4.2 %compare_select_fusion.1 = s32[256,1]{0,1:T(1,128)S(1)} fusion(s32[]{:T(128)} %bitcast.12, s32[]{:T(128)} %bitcast.13, s32[]{:T(128)} %bitcast.14, s32[]{:T(128)} %bitcast.15, s32[]{:T(128)} %bitcast.16, s32[]{:T(128)} %bitcast.18, s32[]{:T(128)} %bitcast.17), kind=kLoop, calls=%fused_computation.35 | loop fusion | flops 5888 | bytes 1052 | tf_op jit(solution)/shard_map/gather | solution.py:66
  158.1 5.6 %fusion.14 = s32[256]{0:T(256)S(1)} fusion(pred[256]{0:T(512)(128)(4,1)S(1)} %get-tuple-element.27, pred[256]{0:T(512)(128)(4,1)S(1)} %get-tuple-element.28, pred[256]{0:T(512)(128)(4,1)S(1)} %get-tuple-element.29, pred[256]{0:T(512)(128)(4,1)S(1)} %get-tuple-element.30, pred[256]{0:T(512)(128)(4,1)S(1)} %get-tuple-element.31, ...), kind=kLoop, calls=%fused_computation.70 | loop fusion | flops 4352 | bytes 4388 | tf_op jit(solution)/shard_map/add | solution.py:66
  163.7 20.1 %all-gather.8.cloned.1.call-done = bf16[1,1024,1024]{2,1,0:T(8,128)(2,1)} async-done(((bf16[1,256,1024]{2,1,0:T(8,128)(2,1)}), bf16[1,1024,1024]{2,1,0:T(8,128)(2,1)}) %all-gather.8.cloned.1.call-update) | async-done | bytes 2097168 | tf_op jit(solution)/shard_map/all_gather | solution.py:30
  183.8 3.3 %copy.6 = bf16[2,16,32,1024]{3,2,1,0:T(8,128)(2,1)} copy(bf16[2,16,32,1024]{3,2,0,1:T(8,128)(2,1)} %bitcast.54) | data formatting | bytes 4194304 | tf_op jit(solution)/shard_map/transpose | solution.py:33
  187.1 23.1 %all-gather.6.cloned.1.call-done = bf16[2048,1024]{0,1:T(8,128)(2,1)} async-done(((bf16[2048,512]{0,1:T(8,128)(2,1)}), bf16[2048,1024]{0,1:T(8,128)(2,1)}) %all-gather.6.cloned.1.call-update) | async-done | bytes 4194320 | tf_op jit(solution)/shard_map/all_gather | solution.py:38
  210.2 7.4 %convolution_convert_fusion = bf16[2048,1024]{1,0:T(8,128)(2,1)S(1)} fusion(bf16[2048,1024]{0,1:T(8,128)(2,1)} %all-gather.6.cloned.1.call-done, bf16[1024,1024]{1,0:T(8,128)(2,1)} %bitcast.55), kind=kOutput, calls=%fused_computation.5 | convolution fusion | flops 4297064448 | bytes 10485760 | tf_op jit(solution)/shard_map/dot_general | solution.py:39
  217.7 13.1 %all_gather.19 = bf16[256,1024]{1,0:T(8,128)(2,1)S(1)} all-gather(bf16[64,1024]{1,0:T(8,128)(2,1)S(1)} %constant_dynamic-slice_fusion), channel_id=1, replica_groups=mesh['front'=4,'row'=4,'z'=16,'core'=2] {'row'}, dimensions={0}, use_global_device_ids=true | all-gather | bytes 655360 | tf_op jit(solution)/shard_map/all_gather | solution.py:45
  231.4 2.3 fusion
  233.7 1.6 convolution_subtract_fusion
  235.3 2.8 %gather_fusion.4 = f32[64,16,256]{2,1,0:T(8,128)} fusion(f32[64,16,256]{2,1,0:T(8,128)} %bitcast.53, s32[1024]{0:T(1024)S(1)} %pad_clamp_fusion), kind=kCustom, calls=%fused_computation.4 | custom fusion | bytes 2097408 | tf_op jit(solution)/shard_map/gather | solution.py:83
  238.2 3.1 %collective-permute-start = (f32[1024,256]{1,0:T(8,128)}, f32[1024,256]{1,0:T(8,128)}, u32[]{:S(2)}, u32[]{:S(2)}) collective-permute-start(f32[1024,256]{1,0:T(8,128)} %bitcast.57), channel_id=1, source_target_pairs={{0,128},{128,0},{256,384},{384,256},{1,129},{129,1},{257,385},{385... | collective-permute-start | bytes 3145736 | tf_op jit(solution)/shard_map/ppermute | solution.py:11
  241.3 2.3 fusion.2
  243.7 1.6 convolution_subtract_fusion.1
  245.3 1.8 gather_fusion.3
  247.1 16.4 %collective-permute-done = f32[1024,256]{1,0:T(8,128)} collective-permute-done((f32[1024,256]{1,0:T(8,128)}, f32[1024,256]{1,0:T(8,128)}, u32[]{:S(2)}, u32[]{:S(2)}) %collective-permute-start) | collective-permute-done | bytes 1048608 | tf_op jit(solution)/shard_map/ppermute | solution.py:11
  263.5 2.3 bitcast_add_fusion
  (34 shorter events, 2.4 us)
Async XLA Ops:
  6.5 227.2 %copy-start = (f32[1,2048,256]{2,1,0:T(8,128)S(1)}, f32[1,2048,256]{2,1,0:T(8,128)}, u32[]{:S(2)}) copy-start(f32[1,2048,256]{2,1,0:T(8,128)} %param.6) | copy-start | bytes 6291460
  9.2 15.5 %copy-start.3 = (bf16[1,8,1024]{2,1,0:T(8,128)(2,1)S(1)}, bf16[1,8,1024]{2,1,0:T(8,128)(2,1)}, u32[]{:S(2)}) copy-start(bf16[1,8,1024]{2,1,0:T(8,128)(2,1)} %param.4) | copy-start | bytes 49156
  9.2 137.2 %all-to-all-start = ((bf16[16,2048,32]{1,2,0:T(8,128)(2,1)}), bf16[16,2048,32]{1,2,0:T(8,128)(2,1)}, u32[]{:S(2)}, u32[]{:S(2)}) async-start(bf16[16,2048,32]{1,2,0:T(8,128)(2,1)} %stack.3), calls=%async_computation | async-start | bytes 4194304 | tf_op jit(solution)/shard_map/all_to_all | solution.py:36
  24.6 122.6 %copy-start.1 = (s32[1,512]{1,0:T(1,128)S(1)}, s32[1,512]{1,0:T(1,128)}, u32[]{:S(2)}) copy-start(s32[1,512]{1,0:T(1,128)} %param.7) | copy-start | bytes 6148
  24.6 159.2 %all-gather.8.cloned.1.call-start = ((), (), s32[]{:S(2)}) async-start(), calls=%async_computation.2 | async-start | bytes 2621440 | tf_op jit(solution)/shard_map/all_gather | solution.py:30
  146.3 63.8 %all-gather.6.cloned.1.call-start = ((), (), s32[]{:S(2)}) async-start(), calls=%async_computation.1 | async-start | bytes 6291456 | tf_op jit(solution)/shard_map/all_gather | solution.py:38
  217.6 13.2 %copy-start.2 = (bf16[2048,1024]{1,0:T(8,128)(2,1)}, bf16[2048,1024]{1,0:T(8,128)(2,1)S(1)}, u32[]{:S(2)}) copy-start(bf16[2048,1024]{1,0:T(8,128)(2,1)S(1)} %convolution_convert_fusion) | copy-start | bytes 12582916
  238.2 25.4 %collective-permute-start = (f32[1024,256]{1,0:T(8,128)}, f32[1024,256]{1,0:T(8,128)}, u32[]{:S(2)}, u32[]{:S(2)}) collective-permute-start(f32[1024,256]{1,0:T(8,128)} %bitcast.57), channel_id=1, source_target_pairs={{0,128},{128,0},{256,384},{384,256},{1,129},{129,1},{257,385},{385... | collective-permute-start | bytes 3145736 | tf_op jit(solution)/shard_map/ppermute | solution.py:11
Sparse Core Ops, SparseCore 0:
  146.5 37.2 all-gather.7
  185.9 24.2 all-gather.5
